TPU v7x, 32 devices: a whole 2x2x4 slice. The times are simulated.
32 devices in a mesh: row: 4 (over y, core), col: 8 (over z, x).
Axes of the slice: x: 2, y: 2, z: 4, core: 2. Of those that a mesh axis runs over, the one named last changes fastest.
Arguments:
- hess: bfloat16 [10, 4, 256, 5, 8, 256], P(None, 'row', None, None, 'col'), may hold values from -6 to 6
- coupling: float32 [32, 256, 2, 256], P(('row', 'col')), may hold values from -6 to 6
- dest_row: int32 [32, 256, 1], P(('row', 'col')), may hold values from 0 to 3, as said below
- local_row: int32 [32, 256], P(('row', 'col')), may hold values from 256 to 2559
- live: int32 [32], P(('row', 'col')), may hold values from 1 to 256, 6144 in all
- pattern: int32 [40, 40], replicated, may hold values 0 or 1
Outputs:
- factor: float32 [10, 4, 256, 5, 8, 256], P(None, 'row', None, None, 'col')
Inputs may be any that keep to these rules, and one draw needn't show every extreme that they name: `dest_row`: among one owner's 256 slots, used or not, one grid row is named exactly 64 times and no grid row more than 64 times. The first live[d] slots of owner d are used; the counts sum to 6144 and one owner uses all 256.
All inputs are finite; a program needn't handle non-finite values. No bound on the sum of `live` on one device may be relied on, other than what follows from the above.
Results may differ from a plain program's by a relative error of at most 0.0003.
Values sent between devices are 32-bit elements; how exact they have to be, the bound alone decides.
No kernel may reach another device: no remote copies, remote signals or barrier semaphores. Data moves between devices by JAX's collectives and lax.ppermute only.
A program may use at most 192 MiB of HBM per device.

v0:
```python
import jax
import jax.numpy as jnp
from jax import lax
from jax.sharding import PartitionSpec as P


def broadcast(value, axis, source):
    kept = jnp.where(lax.axis_index(axis) == source, value, 0).astype(value.dtype)
    return lax.psum(kept, axis)


def symmetric(block):
    return jnp.tril(block) + jnp.swapaxes(jnp.tril(block, -1), -1, -2)


def right_solve(rows, lower_factor):
    return jax.scipy.linalg.solve_triangular(lower_factor, rows.T, lower=True).T


def leading(block00, block10, block11, link):
    size = block00.shape[0]
    first = symmetric(block00)
    second = symmetric(block11)
    coupled = link * block10
    whole = jnp.concatenate(
        [jnp.concatenate([first, coupled.T], 1), jnp.concatenate([coupled, second], 1)], 0
    )
    ident = jnp.eye(2 * size, dtype=whole.dtype)
    spread = jnp.sum(jnp.abs(whole), axis=1) - jnp.abs(jnp.diagonal(whole))
    whole = whole * (1.0 - ident) + ident * (1.0 + spread)[:, None]
    factor00 = jnp.linalg.cholesky(whole[:size, :size])
    factor10 = right_solve(whole[size:, :size], factor00)
    reduced = whole[size:, size:] - jnp.dot(factor10, factor10.T, precision=lax.Precision.HIGHEST)
    factor11 = jnp.linalg.cholesky(reduced)
    return (factor00, factor10, factor11)


def solve_rows(rows, lower_factor):
    result = right_solve(rows, lower_factor)
    return result


def panel_solve(block_rows, f00, f10, f11):
    first = solve_rows(block_rows[:, 0], f00)
    second = solve_rows(
        block_rows[:, 1] - jnp.dot(first, f10.T, precision=lax.Precision.HIGHEST), f11
    )
    return jnp.stack([first, second], 1)


def shards(hess, coupling, dest_row, local_row, live, pattern):
    grid_rows = lax.axis_size("row")
    grid_cols = lax.axis_size("col")
    here_row = lax.axis_index("row")
    here_col = lax.axis_index("col")
    row_blocks = hess.shape[0]
    col_blocks = hess.shape[3]
    block = hess.shape[2]
    slot_count = coupling.shape[1]
    bucket = slot_count // 4
    height = row_blocks * block
    mask = pattern.astype(jnp.float32)
    grid_ids = jnp.arange(grid_rows, dtype=jnp.int32)
    dest = dest_row[0, :, 0]
    active = jnp.arange(slot_count, dtype=jnp.int32) < live[0]
    hits = (dest[:, None] == grid_ids[None, :]) & active[:, None]
    ranks = jnp.cumsum(hits.astype(jnp.int32), axis=0) - 1
    place = jnp.sum(jnp.where(hits, ranks + grid_ids[None, :] * bucket, 0), axis=1)
    place = jnp.where(active, place, grid_rows * bucket)
    outgoing = (
        jnp.zeros((grid_rows * bucket, 2, block), jnp.float32)
        .at[place]
        .set(coupling[0], mode="drop")
    )
    labels = (
        jnp.zeros((grid_rows * bucket,), jnp.float32)
        .at[place]
        .set(local_row[0].astype(jnp.float32), mode="drop")
    )
    arrived, arrived_rows = (
        lax.all_to_all(
            outgoing.reshape(grid_rows, bucket, 2, block),
            "row",
            split_axis=0,
            concat_axis=0,
            tiled=True,
        ),
        lax.all_to_all(
            labels.reshape(grid_rows, bucket), "row", split_axis=0, concat_axis=0, tiled=True
        ),
    )
    partial_value = (
        jnp.zeros((height, 2, block), jnp.float32)
        .at[arrived_rows.astype(jnp.int32).reshape(-1)]
        .add(arrived.reshape(-1, 2, block))
    )
    own = hess[:, 0, :, 0, 0, :].astype(jnp.float32).reshape(height, block)
    which = (jnp.arange(2, dtype=jnp.int32) == here_col).astype(jnp.float32)
    partial_value = partial_value + own[:, None, :] * which[None, :, None]
    corner = hess[0, 0, :, 0, 0, :].astype(jnp.float32)
    at_first = ((here_row == 0) & (here_col == 0)).astype(jnp.float32)
    at_below = ((here_row == 1) & (here_col == 0)).astype(jnp.float32)
    at_second = ((here_row == 1) & (here_col == 1)).astype(jnp.float32)
    pivots = lax.psum(
        jnp.stack([at_first * corner, at_below * corner, at_second * corner]), ("row", "col")
    )
    f00, f10, f11 = leading(pivots[0], pivots[1], pivots[2], mask[1, 0])
    mine = lax.dynamic_index_in_dim(
        mask.reshape(row_blocks, grid_rows, -1), here_row, 1, keepdims=False
    )
    rowmask = jnp.repeat(mine[:, :2], block, axis=0)
    summed = lax.psum(partial_value, "col")
    panel = panel_solve(summed * rowmask[:, :, None], f00, f10, f11)
    head_first = jnp.where(here_row == 0, f00, f10)
    head_second = jnp.where(here_row == 0, jnp.zeros_like(f11), f11)
    head = jnp.stack([head_first, head_second], 1)
    panel = panel.at[:block].set(jnp.where(here_row < 2, head, panel[:block]))
    ratio = grid_cols // grid_rows
    picked = lax.dynamic_index_in_dim(
        panel.reshape(col_blocks, ratio, block, 2, block), here_col // grid_rows, 1, keepdims=False
    )
    across = broadcast(picked, "row", here_col % grid_rows)
    left = panel.reshape(height, 2 * block)
    right = across.reshape(col_blocks * block, 2 * block)
    update = jnp.dot(left, right.T, precision=lax.Precision.HIGHEST).reshape(
        row_blocks, block, col_blocks, block
    )
    tiles = jnp.transpose(hess[:, 0, :, :, 0, :].astype(jnp.float32), (0, 2, 1, 3))
    sym = symmetric(tiles)
    block_i = jnp.arange(row_blocks, dtype=jnp.int32) * grid_rows + here_row
    block_j = jnp.arange(col_blocks, dtype=jnp.int32) * grid_cols + here_col
    links = lax.dynamic_index_in_dim(
        lax.dynamic_index_in_dim(
            mask.reshape(row_blocks, grid_rows, col_blocks, grid_cols), here_row, 1, keepdims=False
        ),
        here_col,
        2,
        keepdims=False,
    )
    same = (block_i[:, None] == block_j[None, :])[:, :, None, None]
    below = (block_i[:, None] > block_j[None, :])[:, :, None, None]
    base = jnp.where(same, sym, jnp.where(below, links[:, :, None, None] * tiles, 0.0))
    trail = base - jnp.transpose(update, (0, 2, 1, 3))
    lower_panel = jnp.transpose(panel.reshape(row_blocks, block, 2, block), (0, 2, 1, 3))
    panel_tile = lax.dynamic_index_in_dim(lower_panel, jnp.minimum(here_col, 1), 1, keepdims=False)
    in_panel = (block_j < 2)[None, :, None, None]
    kept = (block_i[:, None] >= block_j[None, :])[:, :, None, None]
    result = jnp.where(in_panel, panel_tile[:, None], jnp.where(kept, trail, 0.0))
    return jnp.transpose(result, (0, 2, 1, 3)).reshape(row_blocks, 1, block, col_blocks, 1, block)


def solution(mesh):
    return jax.shard_map(
        shards,
        mesh=mesh,
        in_specs=(
            P(None, "row", None, None, "col", None),
            P(("row", "col"), None, None, None),
            P(("row", "col"), None, None),
            P(("row", "col"), None),
            P(("row", "col")),
            P(),
        ),
        out_specs=P(None, "row", None, None, "col", None),
        check_vma=False,
    )
```

profile of v0, /device:TPU:0, one launch (start us, length us, event | category | flops | bytes accessed | tf_op | source)
XLA Modules:
  0.0 492.9 jit_solution(16189000699029080055)
XLA Ops:
  11.0 1.4 scatter_custom_fusion
  13.0 4.3 all-to-all-start
  19.1 9.4 %copy.100 = bf16[10,1,256,5,1,256]{2,5,3,0,4,1:T(8,128)(2,1)} copy(bf16[10,1,256,5,1,256]{5,2,4,3,1,0:T(8,128)(2,1)} %param.11) | data formatting | bytes 13107200 | tf_op args[0]
  28.6 2.5 slice.121
  31.8 1.5 bitcast_convert_fusion
  33.5 4.2 broadcast_multiply_fusion.1
  39.7 24.2 %scatter_fusion = f32[256,2,256]{2,1,0:T(2,128)} fusion(f32[256,2,256]{2,1,0:T(2,128)} %broadcast_in_dim.117, s32[256]{0:T(256)S(1)} %bitcast.222, f32[256,2,256]{2,1,0:T(2,128)S(1)} %bitcast.212), kind=kCustom, calls=%fused_computation.2 | custom fusion | bytes 1573888 | tf_op jit(solution)/shard_map/scatter | solution.py:73
  63.8 3.5 all-to-all-start.1
  67.5 8.7 %all-to-all-done.1 = f32[4,64,2,256]{3,2,1,0:T(2,128)S(1)} async-done(((f32[4,64,2,256]{3,2,1,0:T(2,128)}), f32[4,64,2,256]{3,2,1,0:T(2,128)S(1)}, u32[]{:S(2)}, u32[]{:S(2)}) %all-to-all-start.1) | async-done | bytes 524320 | tf_op jit(solution)/shard_map/all_to_all | solution.py:81
  76.2 30.9 %scatter_fusion.1 = f32[2560,2,256]{2,1,0:T(2,128)} fusion(f32[2560,2,256]{2,1,0:T(2,128)} %broadcast_multiply_fusion.1, s32[256]{0:T(256)S(1)} %bitcast.223, f32[256,2,256]{2,1,0:T(2,128)S(1)} %bitcast.211), kind=kCustom, calls=%fused_computation.3 | custom fusion | flops 131072 | bytes 1573888 | tf_op jit(solution)/shard_map/scatter-add | solution.py:95
  107.1 8.8 %copy.88 = f32[2560,2,256]{0,2,1:T(8,128)} copy(f32[2560,2,256]{2,1,0:T(2,128)} %scatter_fusion.1) | data formatting | bytes 10485760 | tf_op jit(solution)/shard_map/scatter-add | solution.py:95
  116.1 39.1 %all-reduce.5.cloned.1.call-done = f32[3,256,256]{2,1,0:T(8,128)} async-done(((f32[3,256,256]{2,1,0:T(8,128)}), f32[3,256,256]{2,1,0:T(8,128)}) %all-reduce.5.cloned.1.call-update) | async-done | bytes 786448 | tf_op jit(solution)/shard_map/psum | solution.py:104
  156.6 1.7 fusion.29
  158.8 4.5 gather_fusion
  163.8 11.7 %cholesky.130 = f32[128,128]{1,0:T(8,128)S(1)} custom-call(f32[128,128]{1,0:T(8,128)S(1)} %cholesky.194), custom_call_target="Cholesky" | custom-call | tf_op jit(solution)/shard_map/jit(cholesky)/cholesky | solution.py:31
  175.5 9.8 %custom-call.20 = f32[1,128,128]{1,2,0:T(8,128)S(1)} custom-call(f32[1,128,128]{2,1,0:T(8,128)S(1)} %get-tuple-element.87), custom_call_target="InvertDiagBlocksLowerTriangular" | custom-call | tf_op jit(solution)/shard_map/jit(cholesky)/cholesky | solution.py:31
  185.8 11.7 %cholesky.147 = f32[128,128]{1,0:T(8,128)S(1)} custom-call(f32[128,128]{1,0:T(8,128)S(1)} %convolution_subtract_fusion.6), custom_call_target="Cholesky" | custom-call | tf_op jit(solution)/shard_map/jit(cholesky)/cholesky | solution.py:31
  199.6 3.8 while.6
  200.2 1.3 bitcast_dynamic-update-slice_fusion.4
  202.1 1.3 bitcast_dynamic-update-slice_fusion.4
  203.4 20.1 %custom-call.21 = f32[2,128,128]{1,2,0:T(8,128)S(1)} custom-call(f32[2,128,128]{2,1,0:T(8,128)S(1)} %get-tuple-element.41), custom_call_target="InvertDiagBlocksLowerTriangular" | custom-call | tf_op jit(solution)/shard_map/jit(_solve_triangular)/triangular_solve | solution.py:17
  225.2 11.7 %cholesky.164 = f32[128,128]{1,0:T(8,128)S(1)} custom-call(f32[128,128]{1,0:T(8,128)S(1)} %cholesky.197), custom_call_target="Cholesky" | custom-call | tf_op jit(solution)/shard_map/jit(cholesky)/cholesky | solution.py:34
  237.0 9.8 %custom-call.22 = f32[1,128,128]{1,2,0:T(8,128)S(1)} custom-call(f32[1,128,128]{2,1,0:T(8,128)S(1)} %get-tuple-element.83), custom_call_target="InvertDiagBlocksLowerTriangular" | custom-call | tf_op jit(solution)/shard_map/jit(cholesky)/cholesky | solution.py:34
  247.3 11.7 %cholesky.181 = f32[128,128]{1,0:T(8,128)S(1)} custom-call(f32[128,128]{1,0:T(8,128)S(1)} %convolution_subtract_fusion.5), custom_call_target="Cholesky" | custom-call | tf_op jit(solution)/shard_map/jit(cholesky)/cholesky | solution.py:34
  262.3 3.8 while.7
  262.9 1.3 bitcast_dynamic-update-slice_fusion.5
  264.8 1.3 bitcast_dynamic-update-slice_fusion.5
  266.1 20.5 %custom-call.23 = f32[2,128,128]{1,2,0:T(8,128)} custom-call(f32[2,128,128]{2,1,0:T(8,128)S(1)} %get-tuple-element.42), custom_call_target="InvertDiagBlocksLowerTriangular" | custom-call | tf_op jit(solution)/shard_map/jit(_solve_triangular)/triangular_solve | solution.py:17
  287.3 54.9 %all-reduce.7.cloned.1.call-done = f32[2560,2,256]{0,2,1:T(8,128)} async-done(((f32[2560,2,256]{0,2,1:T(8,128)}), f32[2560,2,256]{0,2,1:T(8,128)}) %all-reduce.7.cloned.1.call-update) | async-done | bytes 5242896 | tf_op jit(solution)/shard_map/psum | solution.py:112
  342.2 3.0 broadcast_multiply_fusion
  345.4 2.2 copy-done.1
  348.8 2.3 convolution_subtract_fusion.2
  351.6 3.5 fusion.42
  355.1 4.4 fusion.8
  361.9 2.3 convolution_subtract_fusion.1
  364.2 2.8 copy.97
  368.4 2.4 fusion.34
  372.3 2.2 copy-done
  374.5 2.0 copy.107
  376.5 3.2 dot_general.16
  380.6 11.4 %convert_multiply_fusion = (f32[10,256,5,256]{1,3,2,0:T(8,128)}, f32[10,256,5,256]{1,3,2,0:T(8,128)}) fusion(bf16[10,1,256,5,1,256]{2,5,3,0,4,1:T(8,128)(2,1)} %copy.100, f32[10,5]{1,0:T(8,128)S(1)} %bitcast.215, pred[256,256]{0,1:T(8,128)(4,1)S(1)} %copy-done.9), kind=kLoop, calls=%fused_computation.8 | loop fusion | flops 9830400 | bytes 32833736 | tf_op jit(solution)/shard_map/mul | solution.py:142
  392.0 14.0 %copy.102 = f32[10,256,5,256]{3,1,2,0:T(8,128)} copy(f32[10,256,5,256]{1,3,2,0:T(8,128)} %get-tuple-element.67) | data formatting | bytes 26214400 | tf_op jit(solution)/shard_map/jit(tril)/select_n | solution.py:13
  406.0 14.1 %copy.105 = f32[10,256,5,256]{3,1,2,0:T(8,128)} copy(f32[10,256,5,256]{1,3,2,0:T(8,128)} %get-tuple-element.66) | data formatting | bytes 26214400 | tf_op jit(solution)/shard_map/mul | solution.py:142
  420.3 10.4 %copy.106 = f32[2560,2,256]{2,1,0:T(2,128)} copy(f32[2560,2,256]{2,0,1:T(8,128)} %copy-done) | data formatting | bytes 10485760 | tf_op jit(solution)/shard_map/scatter | solution.py:117
  430.7 8.0 %reshape.409 = f32[10,256,512,1]{2,1,0,3:T(8,128)} reshape(f32[2560,2,256]{2,1,0:T(2,128)} %copy.106) | data formatting | bytes 10485760 | tf_op jit(solution)/shard_map/dot_general | solution.py:125
  438.7 2.0 dynamic-slice_bitcast_fusion
  440.8 30.4 %fusion.6 = f32[10,1,256,5,1,256]{5,2,3,0,4,1:T(8,128)S(1)} fusion(f32[10,256,5,256]{3,1,2,0:T(8,128)} %copy.102, f32[10,256,5,256]{3,1,2,0:T(8,128)} %copy.105, bf16[10,1,256,5,1,256]{2,5,3,0,4,1:T(8,128)(2,1)} %copy.100, f32[10,256,256]{2,1,0:T(8,128)S(1)} %dynamic-slice_bitcast_fusion, pred[5]{0:T(512)(128)(4,1)S(1)} %broadcast_compare_fusion.3, ...), kind=kOutput, calls=%fused_computation.17 | convolution fusion | flops 20158873600 | bytes 56426652 | tf_op jit(solution)/shard_map/dot_general | solution.py:125
  471.2 15.0 %copy.108 = f32[10,1,256,5,1,256]{5,4,3,2,1,0:T(1,128)} copy(f32[10,1,256,5,1,256]{5,2,3,0,4,1:T(8,128)S(1)} %fusion.6) | data formatting | bytes 26214400 | tf_op jit(solution)/shard_map/reshape | solution.py:149
  (128 shorter events, 28.3 us)
Async XLA Ops:
  13.0 50.9 %all-to-all-start = ((f32[4,1,64]{2,1,0:T(1,128)}), f32[4,1,64]{2,1,0:T(1,128)S(1)}, u32[]{:S(2)}, u32[]{:S(2)}) async-start(f32[4,1,64]{2,1,0:T(1,128)} %all_to_all.9), calls=%async_computation | async-start | bytes 4096 | tf_op jit(solution)/shard_map/all_to_all | solution.py:88
  17.2 138.0 %all-reduce.5.cloned.1.call-start = ((), (), s32[]{:S(2)}) async-start(), calls=%async_computation.2 | async-start | bytes 1572864 | tf_op jit(solution)/shard_map/psum | solution.py:104
  28.6 2.5 copy-start.11
  33.5 6.2 %copy-start.8 = (f32[1,256,2,256]{3,2,1,0:T(2,128)S(1)}, f32[1,256,2,256]{3,2,1,0:T(2,128)}, u32[]{:S(2)}) copy-start(f32[1,256,2,256]{3,2,1,0:T(2,128)} %param.12) | copy-start | bytes 1572868
  63.8 12.3 %all-to-all-start.1 = ((f32[4,64,2,256]{3,2,1,0:T(2,128)}), f32[4,64,2,256]{3,2,1,0:T(2,128)S(1)}, u32[]{:S(2)}, u32[]{:S(2)}) async-start(f32[4,64,2,256]{3,2,1,0:T(2,128)} %bitcast.26), calls=%async_computation.1 | async-start | bytes 1048576 | tf_op jit(solution)/shard_map/all_to_all | solution.py:81
  67.4 274.8 %all-reduce.7.cloned.1.call-start = ((), (), s32[]{:S(2)}) async-start(), calls=%async_computation.3 | async-start | bytes 10485760 | tf_op jit(solution)/shard_map/psum | solution.py:112
  115.9 324.9 %all-reduce.9.cloned.1.call-start = ((), (), s32[]{:S(2)}) async-start(), calls=%async_computation.4 | async-start | bytes 5242880 | tf_op jit(solution)/shard_map/psum | solution.py:9
  155.2 3.2 copy-start.5
  345.2 2.4 copy-start.1
  355.1 4.4 copy-start.10
  360.8 1.1 copy-start.2
  367.0 1.3 copy-start.4
  368.4 2.4 copy-start.3
  371.0 1.0 copy-start.6
  371.0 1.0 copy-start.7
  372.1 2.4 copy-start
  379.7 0.8 copy-start.9
Sparse Core Ops, SparseCore 0:
  23.2 131.9 all-reduce.4
  158.9 183.2 all-reduce.6
  379.9 58.9 all-reduce.8
where the time goes:
time: 500 us; the launch traced here: 493 us
  other arithmetic  172 us (34%)
  local copies, waits for them, and re-layouts  143 us (29%)
  waiting for transfers between devices  103 us (21%)
  matrix products  50.3 us (10%)
  between operations  17 us (3%)
  starting transfers between devices  8.02 us (2%)
    psum x1, waiting for transfers between devices, shards(): summed = lax.psum(partial_value, 'col')  54.9 us
    another operation x5, other arithmetic, right_solve(): return jax.scipy.linalg.solve_triangular(lower_factor, rows.T, lower=True).T  40.6 us
    psum x1, waiting for transfers between devices, shards(): lax.psum(jnp.stack([at_first * corner, at_below * corner, at_second * cor...  39.1 us
    another operation x7, other arithmetic, leading(): factor11 = jnp.linalg.cholesky(reduced)  34.6 us
    another operation x6, other arithmetic, leading(): factor00 = jnp.linalg.cholesky(whole[:size, :size])  33.9 us
    scatter-add x1, other arithmetic, shards(): partial_value = jnp.zeros((height, 2, block), jnp.float32).at[arrived_row...  30.9 us
    dot_general x1, matrix products, shards(): jnp.dot(left, right.T, precision=lax.Precision.HIGHEST)  30.4 us
    scatter x1, local copies, waits for them, and re-layouts, shards(): outgoing = jnp.zeros((grid_rows * bucket, 2, block), jnp.float32).at[plac...  24.2 us
  transfers between devices with their start and end apart: 5, of which 3 were waited for; matrix products, arithmetic and copies ran while one was open for 56% of the time, Pallas kernels for 0%

commit v1 on v0

--- a/solution.py
+++ b/solution.py
@@ -109,7 +109,10 @@
         mask.reshape(row_blocks, grid_rows, -1), here_row, 1, keepdims=False
     )
     rowmask = jnp.repeat(mine[:, :2], block, axis=0)
-    summed = lax.psum(partial_value, "col")
+    n_dev, summed = (lax.axis_size("col"), partial_value)
+    for reach in [1 << k for k in range(n_dev.bit_length() - 1)]:
+        swap = [(i, i ^ reach) for i in range(n_dev)]
+        summed = summed + lax.ppermute(summed, "col", swap)
     panel = panel_solve(summed * rowmask[:, :, None], f00, f10, f11)
     head_first = jnp.where(here_row == 0, f00, f10)
     head_second = jnp.where(here_row == 0, jnp.zeros_like(f11), f11)

time: 500 us -> 755 us (1.51)
  waiting for transfers between devices: 103 us -> 337 us
  other arithmetic: 172 us -> 186 us
    ppermute x0 -> x3, waiting for transfers between devices: none -> 214 us  [shards(): summed = summed + lax.ppermute(summed, 'col', swap)]
    psum x1, waiting for transfers between devices: 39.1 us -> 118 us  [shards(): lax.psum(jnp.stack([at_first * corner, at_below * corner, at_second * cor...]
    psum x1 -> x0, waiting for transfers between devices: 54.9 us -> none  [shards(): summed = lax.psum(partial_value, 'col')]
    add x0 -> x2, other arithmetic: none -> 13.1 us  [shards(): summed = summed + lax.ppermute(summed, 'col', swap)]
    unnamed x28 -> x30, local copies, waits for them, and re-layouts: 17.6 us -> 17.9 us
  transfers between devices with their start and end apart: 5 -> 7, of which waited for: 3 -> 4; matrix products, arithmetic and copies ran while one was open for 56% -> 31% of each run, Pallas kernels for 0% -> 0%
where the time goes in v1:
time: 755 us; the launch traced here: 747 us
  waiting for transfers between devices  337 us (45%)
  other arithmetic  186 us (25%)
  local copies, waits for them, and re-layouts  143 us (19%)
  matrix products  50.7 us (7%)
  between operations  17.8 us (2%)
  starting transfers between devices  11.9 us (2%)
    ppermute x3, waiting for transfers between devices, shards(): summed = summed + lax.ppermute(summed, 'col', swap)  214 us
    psum x1, waiting for transfers between devices, shards(): lax.psum(jnp.stack([at_first * corner, at_below * corner, at_second * cor...  118 us
    another operation x5, other arithmetic, right_solve(): return jax.scipy.linalg.solve_triangular(lower_factor, rows.T, lower=True).T  40.7 us
    another operation x7, other arithmetic, leading(): factor11 = jnp.linalg.cholesky(reduced)  34.6 us
    another operation x6, other arithmetic, leading(): factor00 = jnp.linalg.cholesky(whole[:size, :size])  34 us
    scatter-add x1, other arithmetic, shards(): partial_value = jnp.zeros((height, 2, block), jnp.float32).at[arrived_row...  30.9 us
    dot_general x1, matrix products, shards(): jnp.dot(left, right.T, precision=lax.Precision.HIGHEST)  30.4 us
    scatter x1, local copies, waits for them, and re-layouts, shards(): outgoing = jnp.zeros((grid_rows * bucket, 2, block), jnp.float32).at[plac...  24.2 us
  transfers between devices with their start and end apart: 7, of which 4 were waited for; matrix products, arithmetic and copies ran while one was open for 31% of the time, Pallas kernels for 0%

profile of v1, /device:TPU:0, one launch (start us, length us, event | category | flops | bytes accessed | tf_op | source)
XLA Modules:
  0.0 746.5 jit_solution(15402469535359623760)
XLA Ops:
  13.0 4.3 all-to-all-start
  19.8 24.2 %scatter_fusion = f32[256,2,256]{2,1,0:T(2,128)} fusion(f32[256,2,256]{2,1,0:T(2,128)} %broadcast_in_dim.117, s32[256]{0:T(256)S(1)} %bitcast.223, f32[256,2,256]{2,1,0:T(2,128)S(1)} %bitcast.213), kind=kCustom, calls=%fused_computation.2 | custom fusion | bytes 1573888 | tf_op jit(solution)/shard_map/scatter | solution.py:73
  44.0 3.5 all-to-all-start.1
  47.5 4.2 broadcast_multiply_fusion
  51.9 4.5 all-to-all-done.1
  56.3 30.9 %scatter_fusion.1 = f32[2560,2,256]{2,1,0:T(2,128)} fusion(f32[2560,2,256]{2,1,0:T(2,128)} %broadcast_multiply_fusion, s32[256]{0:T(256)S(1)} %bitcast.224, f32[256,2,256]{2,1,0:T(2,128)S(1)} %bitcast.212), kind=kCustom, calls=%fused_computation.3 | custom fusion | flops 131072 | bytes 1573888 | tf_op jit(solution)/shard_map/scatter-add | solution.py:95
  87.2 8.8 %copy.91 = f32[2560,2,256]{0,2,1:T(8,128)} copy(f32[2560,2,256]{2,1,0:T(2,128)} %scatter_fusion.1) | data formatting | bytes 10485760 | tf_op jit(solution)/shard_map/scatter-add | solution.py:95
  96.9 113.3 %collective-permute-done = f32[2560,2,256]{0,2,1:T(8,128)S(1)} collective-permute-done((f32[2560,2,256]{0,2,1:T(8,128)}, f32[2560,2,256]{0,2,1:T(8,128)S(1)}, u32[]{:S(2)}, u32[]{:S(2)}) %collective-permute-start) | collective-permute-done | bytes 5242912 | tf_op jit(solution)/shard_map/ppermute | solution.py:115
  210.2 5.8 add.191
  216.0 1.7 collective-permute-start.1
  219.7 9.5 %copy.103 = bf16[10,1,256,5,1,256]{2,5,3,0,4,1:T(8,128)(2,1)} copy(bf16[10,1,256,5,1,256]{5,2,4,3,1,0:T(8,128)(2,1)} %param.11) | data formatting | bytes 13107200 | tf_op args[0]
  231.2 118.1 %all-reduce.4.cloned.1.call-done = f32[3,256,256]{2,1,0:T(8,128)} async-done(((f32[3,256,256]{2,1,0:T(8,128)}), f32[3,256,256]{2,1,0:T(8,128)}) %all-reduce.4.cloned.1.call-update) | async-done | bytes 786448 | tf_op jit(solution)/shard_map/psum | solution.py:104
  350.7 1.7 fusion.32
  352.9 4.8 gather_fusion
  358.0 7.4 add.192
  365.3 1.4 collective-permute-start.2
  366.8 11.7 %cholesky.130 = f32[128,128]{1,0:T(8,128)S(1)} custom-call(f32[128,128]{1,0:T(8,128)S(1)} %cholesky.194), custom_call_target="Cholesky" | custom-call | tf_op jit(solution)/shard_map/jit(cholesky)/cholesky | solution.py:31
  378.6 9.8 %custom-call.20 = f32[1,128,128]{1,2,0:T(8,128)S(1)} custom-call(f32[1,128,128]{2,1,0:T(8,128)S(1)} %get-tuple-element.87), custom_call_target="InvertDiagBlocksLowerTriangular" | custom-call | tf_op jit(solution)/shard_map/jit(cholesky)/cholesky | solution.py:31
  388.9 11.7 %cholesky.147 = f32[128,128]{1,0:T(8,128)S(1)} custom-call(f32[128,128]{1,0:T(8,128)S(1)} %convolution_subtract_fusion.4), custom_call_target="Cholesky" | custom-call | tf_op jit(solution)/shard_map/jit(cholesky)/cholesky | solution.py:31
  402.8 4.3 while.6
  403.5 1.4 bitcast_dynamic-update-slice_fusion.4
  405.6 1.4 bitcast_dynamic-update-slice_fusion.4
  407.1 20.1 %custom-call.21 = f32[2,128,128]{1,2,0:T(8,128)S(1)} custom-call(f32[2,128,128]{2,1,0:T(8,128)S(1)} %get-tuple-element.41), custom_call_target="InvertDiagBlocksLowerTriangular" | custom-call | tf_op jit(solution)/shard_map/jit(_solve_triangular)/triangular_solve | solution.py:17
  428.9 11.7 %cholesky.164 = f32[128,128]{1,0:T(8,128)S(1)} custom-call(f32[128,128]{1,0:T(8,128)S(1)} %cholesky.197), custom_call_target="Cholesky" | custom-call | tf_op jit(solution)/shard_map/jit(cholesky)/cholesky | solution.py:34
  440.7 9.8 %custom-call.22 = f32[1,128,128]{1,2,0:T(8,128)S(1)} custom-call(f32[1,128,128]{2,1,0:T(8,128)S(1)} %get-tuple-element.83), custom_call_target="InvertDiagBlocksLowerTriangular" | custom-call | tf_op jit(solution)/shard_map/jit(cholesky)/cholesky | solution.py:34
  451.0 11.7 %cholesky.181 = f32[128,128]{1,0:T(8,128)S(1)} custom-call(f32[128,128]{1,0:T(8,128)S(1)} %convolution_subtract_fusion.3), custom_call_target="Cholesky" | custom-call | tf_op jit(solution)/shard_map/jit(cholesky)/cholesky | solution.py:34
  466.2 4.0 while.7
  470.2 20.5 %custom-call.23 = f32[2,128,128]{1,2,0:T(8,128)} custom-call(f32[2,128,128]{2,1,0:T(8,128)S(1)} %get-tuple-element.42), custom_call_target="InvertDiagBlocksLowerTriangular" | custom-call | tf_op jit(solution)/shard_map/jit(_solve_triangular)/triangular_solve | solution.py:17
  491.4 101.1 %collective-permute-done.2 = f32[2560,2,256]{0,2,1:T(8,128)} collective-permute-done((f32[2560,2,256]{0,2,1:T(8,128)}, f32[2560,2,256]{0,2,1:T(8,128)}, u32[]{:S(2)}, u32[]{:S(2)}) %collective-permute-start.2) | collective-permute-done | bytes 5242912 | tf_op jit(solution)/shard_map/ppermute | solution.py:115
  592.5 5.1 add_multiply_fusion
  597.9 2.2 copy-done.1
  601.5 2.3 fusion.46
  604.3 3.9 fusion.15
  608.2 4.4 fusion.9
  615.0 2.3 convolution_subtract_fusion
  617.3 2.8 copy.100
  621.4 2.4 fusion.37
  625.4 2.2 copy-done
  627.6 2.0 copy.110
  629.6 3.2 dot_general.16
  633.7 11.4 %convert_multiply_fusion = (f32[10,256,5,256]{1,3,2,0:T(8,128)}, f32[10,256,5,256]{1,3,2,0:T(8,128)}) fusion(bf16[10,1,256,5,1,256]{2,5,3,0,4,1:T(8,128)(2,1)} %copy.103, f32[10,5]{1,0:T(8,128)S(1)} %bitcast.216, pred[256,256]{0,1:T(8,128)(4,1)S(1)} %copy-done.10), kind=kLoop, calls=%fused_computation.8 | loop fusion | flops 9830400 | bytes 32833736 | tf_op jit(solution)/shard_map/mul | solution.py:145
  645.1 14.0 %copy.105 = f32[10,256,5,256]{3,1,2,0:T(8,128)} copy(f32[10,256,5,256]{1,3,2,0:T(8,128)} %get-tuple-element.67) | data formatting | bytes 26214400 | tf_op jit(solution)/shard_map/jit(tril)/select_n | solution.py:13
  659.1 14.2 %copy.108 = f32[10,256,5,256]{3,1,2,0:T(8,128)} copy(f32[10,256,5,256]{1,3,2,0:T(8,128)} %get-tuple-element.66) | data formatting | bytes 26214400 | tf_op jit(solution)/shard_map/mul | solution.py:145
  673.4 10.4 %copy.109 = f32[2560,2,256]{2,1,0:T(2,128)} copy(f32[2560,2,256]{2,0,1:T(8,128)} %copy-done) | data formatting | bytes 10485760 | tf_op jit(solution)/shard_map/scatter | solution.py:120
  683.8 8.0 %reshape.409 = f32[10,256,512,1]{2,1,0,3:T(8,128)} reshape(f32[2560,2,256]{2,1,0:T(2,128)} %copy.109) | data formatting | bytes 10485760 | tf_op jit(solution)/shard_map/dot_general | solution.py:128
  691.8 2.0 dynamic-slice_bitcast_fusion
  693.8 30.4 %fusion.6 = f32[10,1,256,5,1,256]{5,2,3,0,4,1:T(8,128)S(1)} fusion(f32[10,256,5,256]{3,1,2,0:T(8,128)} %copy.105, f32[10,256,5,256]{3,1,2,0:T(8,128)} %copy.108, bf16[10,1,256,5,1,256]{2,5,3,0,4,1:T(8,128)(2,1)} %copy.103, f32[10,256,256]{2,1,0:T(8,128)S(1)} %dynamic-slice_bitcast_fusion, pred[5]{0:T(512)(128)(4,1)S(1)} %broadcast_compare_fusion.3, ...), kind=kOutput, calls=%fused_computation.17 | convolution fusion | flops 20158873600 | bytes 56426652 | tf_op jit(solution)/shard_map/dot_general | solution.py:128
  724.3 15.0 %copy.111 = f32[10,1,256,5,1,256]{5,4,3,2,1,0:T(1,128)} copy(f32[10,1,256,5,1,256]{5,2,3,0,4,1:T(8,128)S(1)} %fusion.6) | data formatting | bytes 26214400 | tf_op jit(solution)/shard_map/reshape | solution.py:152
  (136 shorter events, 35.3 us)
Async XLA Ops:
  13.0 31.0 %all-to-all-start = ((f32[4,1,64]{2,1,0:T(1,128)}), f32[4,1,64]{2,1,0:T(1,128)S(1)}, u32[]{:S(2)}, u32[]{:S(2)}) async-start(f32[4,1,64]{2,1,0:T(1,128)} %all_to_all.9), calls=%async_computation | async-start | bytes 4096 | tf_op jit(solution)/shard_map/all_to_all | solution.py:88
  17.3 1.3 slice-start
  18.6 1.2 copy-start.9
  44.0 12.3 %all-to-all-start.1 = ((f32[4,64,2,256]{3,2,1,0:T(2,128)}), f32[4,64,2,256]{3,2,1,0:T(2,128)S(1)}, u32[]{:S(2)}, u32[]{:S(2)}) async-start(f32[4,64,2,256]{3,2,1,0:T(2,128)} %bitcast.26), calls=%async_computation.1 | async-start | bytes 1048576 | tf_op jit(solution)/shard_map/all_to_all | solution.py:81
  47.5 301.8 %all-reduce.4.cloned.1.call-start = ((), (), s32[]{:S(2)}) async-start(), calls=%async_computation.2 | async-start | bytes 1572864 | tf_op jit(solution)/shard_map/psum | solution.py:104
  96.0 114.2 %collective-permute-start = (f32[2560,2,256]{0,2,1:T(8,128)}, f32[2560,2,256]{0,2,1:T(8,128)S(1)}, u32[]{:S(2)}, u32[]{:S(2)}) collective-permute-start(f32[2560,2,256]{0,2,1:T(8,128)} %copy.91), channel_id=1, source_target_pairs={{0,1},{1,0},{2,3},{3,2},{4,5},{5,4},{6,7},{7,6},{8,9},{9,8},{10,11... | collective-permute-start | bytes 15728648 | tf_op jit(solution)/shard_map/ppermute | solution.py:115
  216.0 141.9 %collective-permute-start.1 = (f32[2560,2,256]{0,2,1:T(8,128)}, f32[2560,2,256]{0,2,1:T(8,128)}, u32[]{:S(2)}, u32[]{:S(2)}) collective-permute-start(f32[2560,2,256]{0,2,1:T(8,128)} %add.191), channel_id=1, source_target_pairs={{0,2},{1,3},{2,0},{3,1},{4,6},{5,7},{6,4},{7,5},{8,10},{9,11},{10,... | collective-permute-start | bytes 15728648 | tf_op jit(solution)/shard_map/ppermute | solution.py:115
  219.7 9.5 %copy-start.12 = (s32[40,40]{1,0:T(8,128)S(1)}, s32[40,40]{1,0:T(8,128)}, u32[]{:S(2)}) copy-start(s32[40,40]{1,0:T(8,128)} %param.16) | copy-start | bytes 19204
  219.7 474.2 %all-reduce.6.cloned.1.call-start = ((), (), s32[]{:S(2)}) async-start(), calls=%async_computation.3 | async-start | bytes 5242880 | tf_op jit(solution)/shard_map/psum | solution.py:9
  349.3 3.2 copy-start.6
  365.3 227.2 %collective-permute-start.2 = (f32[2560,2,256]{0,2,1:T(8,128)}, f32[2560,2,256]{0,2,1:T(8,128)}, u32[]{:S(2)}, u32[]{:S(2)}) collective-permute-start(f32[2560,2,256]{0,2,1:T(8,128)} %add.192), channel_id=1, source_target_pairs={{0,4},{1,5},{2,6},{3,7},{4,0},{5,1},{6,2},{7,3},{8,12},{9,13},{10,... | collective-permute-start | bytes 15728648 | tf_op jit(solution)/shard_map/ppermute | solution.py:115
  597.7 2.4 copy-start.1
  600.0 1.5 copy-start.3
  608.2 4.4 copy-start.11
  613.9 1.1 copy-start.2
  620.1 1.3 copy-start.5
  621.4 2.4 copy-start.4
  624.1 1.0 copy-start.7
  624.1 1.0 copy-start.8
  625.2 2.4 copy-start
  632.8 0.8 copy-start.10
Sparse Core Ops, SparseCore 0:
  219.8 129.4 all-reduce.3
  633.0 58.6 all-reduce.5
